TPU v7x, 256 devices: a whole 4x4x8 slice. The times are simulated.
256 devices in a mesh: req: 32 (over y, x, core), tp: 8 (over z).
Axes of the slice: x: 4, y: 4, z: 8, core: 2. Of those that a mesh axis runs over, the one named last changes fastest.
Arguments:
- tokens: bfloat16 [256, 4, 1536], P('req'), may hold values from -6 to 6
- lengths: int32 [256], P('req'), may hold values from 16 to 32768, as said below
- page_table: int32 [256, 9], P('req'), may hold values from 0 to 2303, as said below
- kv_pages: bfloat16 [2304, 2, 128, 128], P('req'), may hold values from -480 to 480
- norm_gain: float32 [1536], replicated, may hold values from 0.1 to 1.9
- query_weight: bfloat16 [1536, 1024], P(None, 'tp'), may hold values from -0.15625 to 0.15625
- key_weight: bfloat16 [1536, 128], replicated, may hold values from -0.15625 to 0.15625
- value_weight: bfloat16 [1536, 128], replicated, may hold values from -0.15625 to 0.15625
- out_weight: bfloat16 [1024, 1536], P('tp'), may hold values from -0.1875 to 0.1875
- mlp_gain: float32 [1536], replicated, may hold values from 0.1 to 1.9
- gate_weight: bfloat16 [1536, 4608], P(None, 'tp'), may hold values from -0.15625 to 0.15625
- up_weight: bfloat16 [1536, 4608], P(None, 'tp'), may hold values from -0.15625 to 0.15625
- down_weight: bfloat16 [4608, 1536], P('tp'), may hold values from -0.09375 to 0.09375
Outputs:
- layer_out: bfloat16 [256, 4, 1536], P('req')
Inputs may be any that keep to these rules, and one draw needn't show every extreme that they name: `lengths`: one request has exactly 32768 cached positions in every draw. `page_table`: all entries together are a permutation of the 2304 pool pages. Entry (r, j) is pool page r * 9 + j, in the part of the pool held with request r, except for spilled entries chosen from the seed (about a fifth of all); the spilled entries hold one another's pool pages in an order drawn from the seed, mostly on other devices of req.
All inputs are finite; a program needn't handle non-finite values.
Results may differ from a plain program's by a relative error of at most 0.0095.
The roundings to bfloat16 on the way count: a program that leaves them out, or rounds other values in their place, can miss the bound.
Values may be sent and summed in bfloat16 or wider, within the bound.
No kernel may reach another device: no remote copies, remote signals or barrier semaphores. Data moves between devices by JAX's collectives and lax.ppermute only.
A program may use at most 128 MiB of HBM per device.

v0:
```python
import jax
import jax.numpy as jnp
from jax import lax
from jax.sharding import PartitionSpec as P

WINDOW = 1024
negative = -1e30
epsilon = 1e-06


def rms_norm(values, gain):
    return values * lax.rsqrt(jnp.mean(values * values, axis=-1, keepdims=True) + epsilon) * gain


def body(
    tokens,
    lengths,
    page_table,
    kv_pages,
    norm_gain,
    query_weight,
    key_weight,
    value_weight,
    out_weight,
    mlp_gain,
    gate_weight,
    up_weight,
    down_weight,
):
    req_dev, steps, width = tokens.shape
    head_dim = key_weight.shape[1]
    heads_dev = query_weight.shape[1] // head_dim
    pool_size = kv_pages.shape[0]
    page_size = kv_pages.shape[2]
    window_pages = page_table.shape[1]
    token_rows = tokens.reshape(req_dev * steps, width)
    normed = rms_norm(token_rows.astype(jnp.float32), norm_gain).astype(jnp.bfloat16)
    queries = (
        jnp.dot(normed, query_weight, preferred_element_type=jnp.float32) * head_dim ** (-0.5)
    ).astype(jnp.bfloat16)
    key_new = jnp.dot(normed, key_weight, preferred_element_type=jnp.float32).astype(jnp.bfloat16)
    value_new = jnp.dot(normed, value_weight, preferred_element_type=jnp.float32).astype(
        jnp.bfloat16
    )
    all_lengths, all_table = (
        lax.all_gather(lengths, "req", axis=0, tiled=True),
        lax.all_gather(page_table, "req", axis=0, tiled=True),
    )
    all_queries = lax.all_gather(
        queries.reshape(req_dev, steps, heads_dev * head_dim), "req", axis=0, tiled=True
    )
    requests = all_lengths.shape[0]
    flat_table = all_table.reshape(-1)
    local_slot = flat_table - lax.axis_index("req") * pool_size
    inside = (local_slot >= 0) & (local_slot < pool_size)
    owner_entry = (
        jnp.zeros((pool_size,), jnp.int32)
        .at[jnp.where(inside, local_slot, pool_size)]
        .set(jnp.arange(flat_table.shape[0], dtype=jnp.int32), mode="drop")
    )
    page_request = owner_entry // window_pages
    page_number = owner_entry % window_pages
    page_length = all_lengths[page_request]
    first_page = jnp.maximum(page_length - (WINDOW - 1), 0) // page_size
    position = (first_page + page_number)[:, None] * page_size + jnp.arange(
        page_size, dtype=jnp.int32
    )[None, :]
    current = page_length[:, None] + jnp.arange(steps, dtype=jnp.int32)[None, :]
    visible = (position[:, None, :] < page_length[:, None, None]) & (
        position[:, None, :] > current[:, :, None] - WINDOW
    )
    visible = visible[:, :, None, :]
    page_queries = all_queries[page_request]
    scores = jnp.einsum(
        "pqd,pkd->pqk", page_queries, kv_pages[:, 0], preferred_element_type=jnp.float32
    )
    scores = jnp.where(visible, scores.reshape(pool_size, steps, heads_dev, page_size), negative)
    block_max = jnp.max(scores, axis=-1)
    weights = jnp.where(visible, jnp.exp(scores - block_max[..., None]), 0.0)
    block_total = jnp.sum(weights, axis=-1)
    block_out = jnp.einsum(
        "pqk,pkd->pqd",
        weights.astype(jnp.bfloat16).reshape(pool_size, steps * heads_dev, page_size),
        kv_pages[:, 1],
        preferred_element_type=jnp.float32,
    )
    block_out = block_out.reshape(pool_size, steps, heads_dev, head_dim)
    request_max = jnp.maximum(
        jax.ops.segment_max(block_max, page_request, num_segments=requests), negative
    )
    start_row = lax.axis_index("req") * req_dev
    cache_max = lax.pmax(request_max, "req")
    scale = jnp.exp(block_max - cache_max[page_request])
    sent_out = jax.ops.segment_sum(
        block_out * scale[..., None], page_request, num_segments=requests
    )
    sent_total = jax.ops.segment_sum(block_total * scale, page_request, num_segments=requests)
    cache_out, cache_total = (
        lax.psum_scatter(sent_out, "req", scatter_dimension=0, tiled=True),
        lax.psum_scatter(sent_total, "req", scatter_dimension=0, tiled=True),
    )
    mine_max = lax.dynamic_slice_in_dim(cache_max, start_row, req_dev, 0)
    local_queries = queries.reshape(req_dev, steps, heads_dev, head_dim)
    new_scores = jnp.einsum(
        "rshd,rtd->rsht",
        local_queries,
        key_new.reshape(req_dev, steps, head_dim),
        preferred_element_type=jnp.float32,
    )
    causal = (jnp.arange(steps)[None, :] <= jnp.arange(steps)[:, None])[None, :, None, :]
    new_scores = jnp.where(causal, new_scores, negative)
    new_max = jnp.max(new_scores, axis=-1)
    new_weights = jnp.where(causal, jnp.exp(new_scores - new_max[..., None]), 0.0)
    new_total = jnp.sum(new_weights, axis=-1)
    new_out = jnp.einsum(
        "rsht,rtd->rshd",
        new_weights.astype(jnp.bfloat16),
        value_new.reshape(req_dev, steps, head_dim),
        preferred_element_type=jnp.float32,
    )
    overall = jnp.maximum(mine_max, new_max)
    cache_scale = jnp.exp(mine_max - overall)
    new_scale = jnp.exp(new_max - overall)
    total = cache_total * cache_scale + new_total * new_scale
    summed = cache_out * cache_scale[..., None] + new_out * new_scale[..., None]
    attended = (
        (summed / total[..., None])
        .astype(jnp.bfloat16)
        .reshape(req_dev * steps, heads_dev * head_dim)
    )
    projected = jnp.dot(attended, out_weight, preferred_element_type=jnp.float32)
    attn_total = lax.psum(projected, "tp")
    residual = (token_rows.astype(jnp.float32) + attn_total).astype(jnp.bfloat16)
    mlp_in = rms_norm(residual.astype(jnp.float32), mlp_gain).astype(jnp.bfloat16)
    gate = jnp.dot(mlp_in, gate_weight, preferred_element_type=jnp.float32)
    upward = jnp.dot(mlp_in, up_weight, preferred_element_type=jnp.float32)
    hidden = (jax.nn.gelu(gate, approximate=True) * upward).astype(jnp.bfloat16)
    mlp_total = lax.psum(
        jnp.dot(hidden, down_weight, preferred_element_type=jnp.float32).astype(jnp.bfloat16), "tp"
    ).astype(jnp.float32)
    layer_out = (residual.astype(jnp.float32) + mlp_total).astype(jnp.bfloat16)
    return layer_out.reshape(req_dev, steps, width)


def solution(mesh):
    return jax.shard_map(
        body,
        mesh=mesh,
        in_specs=(
            P("req", None, None),
            P("req"),
            P("req", None),
            P("req", None, None, None),
            P(),
            P(None, "tp"),
            P(),
            P(),
            P("tp", None),
            P(),
            P(None, "tp"),
            P(None, "tp"),
            P("tp", None),
        ),
        out_specs=P("req", None, None),
        check_vma=False,
    )
```

profile of v0, /device:TPU:2, one launch (start us, length us, event | category | flops | bytes accessed | tf_op | source)
XLA Modules:
  0.0 512.9 jit_solution(16299514413610461038)
XLA Ops:
  6.5 0.0 copy-start
  6.5 0.0 reduce-scatter.6.cloned.1.call-start
  6.5 1.4 fusion.63
  8.6 0.9 dynamic-update-slice
  9.5 15.7 %all-reduce = s32[256]{0:T(256)S(1)} all-reduce(s32[256]{0:T(256)S(1)} %dynamic-update-slice), channel_id=1, replica_groups=mesh['req'=32,'tp'=8] {'req'}, use_global_device_ids=true, to_apply=%add | all-reduce | flops 256 | bytes 2048
  25.2 23.4 %all_gather.9 = s32[256,9]{1,0:T(8,128)S(1)} all-gather(s32[8,9]{1,0:T(8,128)} %param.15), channel_id=1, replica_groups=mesh['req'=32,'tp'=8] {'req'}, dimensions={0}, use_global_device_ids=true | all-gather | bytes 9504 | tf_op jit(solution)/shard_map/all_gather | solution.py:47
  48.5 0.2 sub.78
  48.8 9.0 %scatter_custom_fusion = s32[72]{0:T(128)S(1)} fusion(s32[2304]{0:T(1024)S(1)} %fusion.44, s32[2304]{0:T(1024)S(1)} %iota.34, s32[]{:T(128)} %constant.27.clone.1), kind=kCustom, calls=%fused_computation.93 | custom fusion | bytes 292 | tf_op jit(solution)/shard_map/scatter | solution.py:59
  57.8 1.3 gather_fusion
  59.1 0.1 broadcast_compare_fusion
  59.2 0.0 copy-start.8
  59.2 0.1 iota_add_fusion
  59.3 0.1 add_add_fusion
  59.4 1.0 multiply_reduce_fusion
  60.4 0.9 reshape.246
  61.4 0.1 rsqrt.20
  61.4 0.8 multiply_convert_fusion
  62.2 0.0 copy-done.2
  62.2 0.2 fusion.14
  62.4 22.6 %all_gather.11 = bf16[256,4,128]{2,1,0:T(4,128)(2,1)S(1)} all-gather(bf16[8,4,128]{2,1,0:T(4,128)(2,1)S(1)} %bitcast.89), channel_id=1, replica_groups=mesh['req'=32,'tp'=8] {'req'}, dimensions={0}, use_global_device_ids=true | all-gather | bytes 270336 | tf_op jit(solution)/shard_map/all_gather | solution.py:49
  85.0 0.7 gather_fusion.1
  85.7 3.1 fusion.64
  88.8 1.0 scatter_custom_fusion.1
  89.8 123.3 %pmax.7 = f32[256,4,1]{1,0,2:T(8,128)S(1)} all-reduce(f32[256,4,1]{1,0,2:T(8,128)S(1)} %maximum_bitcast_fusion), channel_id=1, replica_groups=mesh['req'=32,'tp'=8] {'req'}, use_global_device_ids=true, to_apply=%region_4.5 | all-reduce | flops 1024 | bytes 8192 | tf_op jit(solution)/shard_map/pmax | solution.py:92
  213.1 0.6 gather_fusion.2
  213.7 0.0 copy-start.6
  213.8 0.0 copy-done.8
  213.8 0.0 copy-done.4
  213.8 2.5 fusion.9
  216.3 0.1 broadcast.190
  216.3 0.0 copy-done.6
  216.3 3.5 scatter_fusion
  219.8 0.0 copy-start.1
  219.8 0.8 copy.86
  220.7 0.0 reduce-scatter.6.cloned.1.call-update
  220.7 0.0 copy-start.9
  220.7 0.0 all-reduce.5.cloned.1.call-start
  220.8 0.0 copy-done.3
  220.8 0.2 convolution_convert_fusion.2
  221.0 0.1 fusion.65
  221.1 0.1 copy.56
  221.2 0.1 select_reduce_fusion
  221.3 0.1 copy.59
  221.4 0.1 fusion.45
  221.5 0.1 copy.81
  221.6 0.1 copy.63
  221.7 1.3 fusion.57
  222.9 1.2 scatter_custom_fusion.3
  224.7 123.8 %all-reduce.1 = f32[256,4,1]{1,0,2:T(8,128)S(1)} all-reduce(f32[256,4,1]{1,0,2:T(8,128)S(1)} %bitcast.88), channel_id=3, replica_groups=mesh['req'=32,'tp'=8] {'req'}, use_global_device_ids=true, to_apply=%region_10.11.clone | all-reduce | flops 1024 | bytes 8192
  348.6 1.2 convolution_convert_fusion.1
  349.8 0.0 reduce-scatter.6.cloned.1.call-done
  349.8 0.7 reshape.332
  350.5 0.1 fusion.17
  350.7 0.9 fusion.66
  351.5 0.0 all-reduce.5.cloned.1.call-update
  351.6 0.0 all-reduce.7.cloned.1.call-start
  351.6 75.7 %all-reduce.5.cloned.1.call-done = f32[32,1536]{1,0:T(8,128)} async-done(((f32[32,1536]{1,0:T(8,128)}), f32[32,1536]{1,0:T(8,128)}) %all-reduce.5.cloned.1.call-update) | async-done | bytes 196624 | tf_op jit(solution)/shard_map/psum | solution.py:132
  427.3 1.1 fusion.18
  428.4 2.1 fusion.42
  430.5 3.2 convolution_convert_fusion
  433.7 0.0 all-reduce.7.cloned.1.call-update
  433.7 71.0 %all-reduce.7.cloned.1.call-done = bf16[32,1536]{1,0:T(8,128)(2,1)} async-done(((bf16[32,1536]{1,0:T(8,128)(2,1)}), bf16[32,1536]{1,0:T(8,128)(2,1)}) %all-reduce.7.cloned.1.call-update) | async-done | bytes 98320 | tf_op jit(solution)/shard_map/psum | solution.py:138
  504.8 0.9 fusion.21
  505.7 0.7 reshape.245
  (23 shorter events, 0.2 us)
Async XLA Ops:
  6.5 424.0 %copy-start = (bf16[576,1536]{1,0:T(8,128)(2,1)S(1)}, bf16[576,1536]{1,0:T(8,128)(2,1)}, u32[]{:S(2)}) copy-start(bf16[576,1536]{1,0:T(8,128)(2,1)} %param.25) | copy-start | bytes 5308420
  6.5 55.7 %copy-start.2 = (bf16[1536,128]{1,0:T(8,128)(2,1)S(1)}, bf16[1536,128]{1,0:T(8,128)(2,1)}, u32[]{:S(2)}) copy-start(bf16[1536,128]{1,0:T(8,128)(2,1)} %param.18) | copy-start | bytes 1179652
  6.5 343.3 %reduce-scatter.6.cloned.1.call-start = ((), (), s32[]{:S(2)}) async-start(), calls=%async_computation.3 | async-start | bytes 540672
  59.2 154.5 %copy-start.8 = (pred[72,128]{1,0:T(8,128)(4,1)}, pred[72,128]{1,0:T(8,128)(4,1)S(1)}, u32[]{:S(2)}) copy-start(pred[72,128]{1,0:T(8,128)(4,1)S(1)} %broadcast_compare_fusion) | copy-start | bytes 27652
  59.3 154.5 %copy-start.4 = (s32[72,128]{1,0:T(8,128)}, s32[72,128]{1,0:T(8,128)S(1)}, u32[]{:S(2)}) copy-start(s32[72,128]{1,0:T(8,128)S(1)} %iota_add_fusion) | copy-start | bytes 110596
  59.4 154.4 %copy-start.5 = (s32[72,4]{1,0:T(8,128)}, s32[72,4]{1,0:T(8,128)S(1)}, u32[]{:S(2)}) copy-start(s32[72,4]{1,0:T(8,128)S(1)} %add_add_fusion) | copy-start | bytes 3460
  88.8 125.0 %copy-start.7 = (f32[72,4,128]{2,1,0:T(4,128)}, f32[72,4,128]{2,1,0:T(4,128)S(1)}, u32[]{:S(2)}) copy-start(f32[72,4,128]{2,1,0:T(4,128)S(1)} %get-tuple-element.17) | copy-start | bytes 442372
  213.7 2.6 copy-start.6
  216.3 4.5 copy-start.3
  219.8 130.8 %copy-start.1 = (bf16[128,1536]{1,0:T(8,128)(2,1)S(1)}, bf16[128,1536]{1,0:T(8,128)(2,1)}, u32[]{:S(2)}) copy-start(bf16[128,1536]{1,0:T(8,128)(2,1)} %param.21) | copy-start | bytes 1179652
  220.7 207.7 %copy-start.9 = (f32[1536]{0:T(1024)S(1)}, f32[1536]{0:T(1024)}, u32[]{:S(2)}) copy-start(f32[1536]{0:T(1024)} %param.22) | copy-start | bytes 18436
  220.7 206.6 %all-reduce.5.cloned.1.call-start = ((), (), s32[]{:S(2)}) async-start(), calls=%async_computation.1 | async-start | bytes 393216 | tf_op jit(solution)/shard_map/psum | solution.py:132
  351.6 153.2 %all-reduce.7.cloned.1.call-start = ((), (), s32[]{:S(2)}) async-start(), calls=%async_computation.2 | async-start | bytes 196608 | tf_op jit(solution)/shard_map/psum | solution.py:138
Sparse Core Ops, SparseCore 0:
  220.8 87.7 reduce-scatter.5
  351.7 75.5 all-reduce.4
  433.8 70.8 all-reduce.6
where the time goes:
time: 514 us; the launch traced here: 513 us
  blocking collectives  309 us (60%)
  waiting for transfers between devices  147 us (29%)
  local copies, waits for them, and re-layouts  17.7 us (3%)
  between operations  14.6 us (3%)
  matrix products  13.5 us (3%)
  other arithmetic  11.4 us (2%)
    unnamed x2, blocking collectives  140 us
    pmax x1, blocking collectives, body(): cache_max = lax.pmax(request_max, 'req')  123 us
    psum x1, waiting for transfers between devices, body(): attn_total = lax.psum(projected, 'tp')  75.7 us
    psum x1, waiting for transfers between devices, body(): lax.psum(jnp.dot(hidden, down_weight, preferred_element_type=jnp.float32)...  71 us
    all_gather x1, blocking collectives, body(): lax.all_gather(page_table, 'req', axis=0, tiled=True)  23.4 us
    all_gather x1, blocking collectives, body(): lax.all_gather(queries.reshape(req_dev, steps, heads_dev * head_dim), 're...  22.6 us
  transfers between devices with their start and end apart: 3, of which 2 were waited for; matrix products, arithmetic and copies ran while one was open for 1% of the time, Pallas kernels for 0%

commit v1 on v0

--- a/solution.py
+++ b/solution.py
@@ -129,7 +129,13 @@
         .reshape(req_dev * steps, heads_dev * head_dim)
     )
     projected = jnp.dot(attended, out_weight, preferred_element_type=jnp.float32)
-    attn_total = lax.psum(projected, "tp")
+    count = lax.axis_size("tp")
+    attn_total, hop = (projected, 1)
+    while hop < count:
+        attn_total = attn_total + lax.ppermute(
+            attn_total, "tp", [(i, i ^ hop) for i in range(count)]
+        )
+        hop = 2 * hop
     residual = (token_rows.astype(jnp.float32) + attn_total).astype(jnp.bfloat16)
     mlp_in = rms_norm(residual.astype(jnp.float32), mlp_gain).astype(jnp.bfloat16)
     gate = jnp.dot(mlp_in, gate_weight, preferred_element_type=jnp.float32)

time: 514 us -> 475 us (0.924)
  waiting for transfers between devices: 147 us -> 93.2 us
  starting transfers between devices: 0.09 us -> 11.5 us
    psum x1 -> x0, waiting for transfers between devices: 75.7 us -> none  [body(): attn_total = lax.psum(projected, 'tp')]
    ppermute x0 -> x3, waiting for transfers between devices: none -> 19 us  [body(): lax.ppermute(attn_total, 'tp', [(i, i ^ hop) for i in range(count)])]
    ppermute x0 -> x3, starting transfers between devices: none -> 11.5 us  [body(): lax.ppermute(attn_total, 'tp', [(i, i ^ hop) for i in range(count)])]
  transfers between devices with their start and end apart: 3 -> 5, of which waited for: 2 -> 4; matrix products, arithmetic and copies ran while one was open for 1% -> 1% of each run, Pallas kernels for 0% -> 0%
where the time goes in v1:
time: 475 us; the launch traced here: 474 us
  blocking collectives  310 us (65%)
  waiting for transfers between devices  93.2 us (20%)
  local copies, waits for them, and re-layouts  19.6 us (4%)
  between operations  15.1 us (3%)
  matrix products  13.8 us (3%)
  starting transfers between devices  11.5 us (2%)
  other arithmetic  11.2 us (2%)
    unnamed x2, blocking collectives  141 us
    pmax x1, blocking collectives, body(): cache_max = lax.pmax(request_max, 'req')  123 us
    psum x1, waiting for transfers between devices, body(): lax.psum(jnp.dot(hidden, down_weight, preferred_element_type=jnp.float32)...  74.1 us
    all_gather x1, blocking collectives, body(): lax.all_gather(page_table, 'req', axis=0, tiled=True)  23.4 us
    all_gather x1, blocking collectives, body(): lax.all_gather(queries.reshape(req_dev, steps, heads_dev * head_dim), 're...  22.6 us
    ppermute x3, waiting for transfers between devices, body(): lax.ppermute(attn_total, 'tp', [(i, i ^ hop) for i in range(count)])  19 us
    ppermute x3, starting transfers between devices, body(): lax.ppermute(attn_total, 'tp', [(i, i ^ hop) for i in range(count)])  11.5 us
  transfers between devices with their start and end apart: 5, of which 4 were waited for; matrix products, arithmetic and copies ran while one was open for 1% of the time, Pallas kernels for 0%

profile of v1, /device:TPU:2, one launch (start us, length us, event | category | flops | bytes accessed | tf_op | source)
XLA Modules:
  0.0 474.2 jit_solution(17992276218561833858)
XLA Ops:
  6.5 0.0 copy-start
  6.5 1.5 fusion.63
  8.7 0.9 dynamic-update-slice
  9.5 15.7 %all-reduce = s32[256]{0:T(256)S(1)} all-reduce(s32[256]{0:T(256)S(1)} %dynamic-update-slice), channel_id=1, replica_groups=mesh['req'=32,'tp'=8] {'req'}, use_global_device_ids=true, to_apply=%add | all-reduce | flops 256 | bytes 2048
  25.2 23.4 %all_gather.9 = s32[256,9]{1,0:T(8,128)S(1)} all-gather(s32[8,9]{1,0:T(8,128)} %param.15), channel_id=1, replica_groups=mesh['req'=32,'tp'=8] {'req'}, dimensions={0}, use_global_device_ids=true | all-gather | bytes 9504 | tf_op jit(solution)/shard_map/all_gather | solution.py:47
  48.6 0.2 sub.78
  48.8 9.0 %scatter_custom_fusion = s32[72]{0:T(128)S(1)} fusion(s32[2304]{0:T(1024)S(1)} %fusion.44, s32[2304]{0:T(1024)S(1)} %iota.34, s32[]{:T(128)} %constant.27.clone.1), kind=kCustom, calls=%fused_computation.93 | custom fusion | bytes 292 | tf_op jit(solution)/shard_map/scatter | solution.py:59
  57.9 1.3 gather_fusion
  59.1 0.1 broadcast_compare_fusion
  59.2 0.1 iota_add_fusion
  59.3 0.1 add_add_fusion
  59.4 1.0 multiply_reduce_fusion
  60.4 0.9 reshape.246
  61.4 0.1 rsqrt.20
  61.4 0.8 multiply_convert_fusion
  62.2 0.0 copy-start.6
  62.3 0.2 fusion.14
  62.4 22.6 %all_gather.11 = bf16[256,4,128]{2,1,0:T(4,128)(2,1)S(1)} all-gather(bf16[8,4,128]{2,1,0:T(4,128)(2,1)S(1)} %bitcast.89), channel_id=1, replica_groups=mesh['req'=32,'tp'=8] {'req'}, dimensions={0}, use_global_device_ids=true | all-gather | bytes 270336 | tf_op jit(solution)/shard_map/all_gather | solution.py:49
  85.1 0.7 gather_fusion.1
  85.7 3.1 fusion.64
  88.8 1.0 scatter_custom_fusion.1
  89.8 123.3 %pmax.7 = f32[256,4,1]{1,0,2:T(8,128)S(1)} all-reduce(f32[256,4,1]{1,0,2:T(8,128)S(1)} %maximum_bitcast_fusion), channel_id=1, replica_groups=mesh['req'=32,'tp'=8] {'req'}, use_global_device_ids=true, to_apply=%region_4.5 | all-reduce | flops 1024 | bytes 8192 | tf_op jit(solution)/shard_map/pmax | solution.py:92
  213.1 0.6 gather_fusion.2
  213.8 0.0 copy-done.7
  213.8 2.5 fusion.9
  216.2 0.1 broadcast.190
  216.3 3.5 scatter_fusion
  219.8 0.8 copy.86
  220.6 0.0 reduce-scatter.6.cloned.1.call-update
  220.6 0.0 all-reduce.4.cloned.1.call-start
  220.7 0.2 convolution_convert_fusion.2
  220.9 0.1 fusion.65
  221.0 0.1 copy.56
  221.1 0.1 select_reduce_fusion
  221.2 0.1 copy.59
  221.3 0.1 fusion.45
  221.4 0.1 copy.81
  221.5 0.7 copy.63
  222.2 0.3 fusion.57
  222.6 1.6 scatter_custom_fusion.3
  224.9 125.0 %all-reduce.1 = f32[256,4,1]{1,0,2:T(8,128)} all-reduce(f32[256,4,1]{1,0,2:T(8,128)} %bitcast.88), channel_id=3, replica_groups=mesh['req'=32,'tp'=8] {'req'}, use_global_device_ids=true, to_apply=%region_10.11.clone | all-reduce | flops 1024 | bytes 8192
  349.9 1.3 fusion.52
  351.2 1.2 convolution_convert_fusion.1
  352.5 0.0 reduce-scatter.6.cloned.1.call-done
  352.5 1.3 reshape.332
  353.8 0.9 fusion.17
  354.7 1.2 fusion.66
  355.9 2.1 collective-permute-start
  357.9 5.4 %collective-permute-done = f32[32,1536]{1,0:T(8,128)S(1)} collective-permute-done((f32[32,1536]{1,0:T(8,128)S(1)}, f32[32,1536]{1,0:T(8,128)S(1)}, u32[]{:S(2)}, u32[]{:S(2)}) %collective-permute-start) | collective-permute-done | bytes 196640 | tf_op jit(solution)/shard_map/ppermute | solution.py:135
  363.3 3.0 collective-permute-start.1
  366.3 10.0 %collective-permute-done.1 = f32[32,1536]{1,0:T(8,128)S(1)} collective-permute-done((f32[32,1536]{1,0:T(8,128)S(1)}, f32[32,1536]{1,0:T(8,128)S(1)}, u32[]{:S(2)}, u32[]{:S(2)}) %collective-permute-start.1) | collective-permute-done | bytes 196640 | tf_op jit(solution)/shard_map/ppermute | solution.py:135
  376.3 6.4 %collective-permute-start.2 = (f32[32,1536]{1,0:T(8,128)S(1)}, f32[32,1536]{1,0:T(8,128)S(1)}, u32[]{:S(2)}, u32[]{:S(2)}) collective-permute-start(f32[32,1536]{1,0:T(8,128)S(1)} %add.145), channel_id=1, source_target_pairs={{0,4},{1,5},{2,6},{3,7},{4,0},{5,1},{6,2},{7,3},{8,12},{9,13},{10,... | collective-permute-start | bytes 589832 | tf_op jit(solution)/shard_map/ppermute | solution.py:135
  382.7 3.6 collective-permute-done.2
  386.4 0.1 fusion.18
  386.5 0.6 copy-done.4
  387.2 0.0 copy-done.10
  387.2 1.3 fusion.42
  388.5 0.0 copy-done
  388.5 3.2 convolution_convert_fusion
  391.6 0.0 all-reduce.4.cloned.1.call-update
  391.7 74.1 %all-reduce.4.cloned.1.call-done = bf16[32,1536]{1,0:T(8,128)(2,1)} async-done(((bf16[32,1536]{1,0:T(8,128)(2,1)}), bf16[32,1536]{1,0:T(8,128)(2,1)}) %all-reduce.4.cloned.1.call-update) | async-done | bytes 98320 | tf_op jit(solution)/shard_map/psum | solution.py:144
  465.8 0.0 copy-done.5
  465.8 0.9 fusion.21
  466.7 0.7 reshape.245
  (30 shorter events, 0.2 us)
Async XLA Ops:
  6.5 381.9 %copy-start = (bf16[576,1536]{1,0:T(8,128)(2,1)S(1)}, bf16[576,1536]{1,0:T(8,128)(2,1)}, u32[]{:S(2)}) copy-start(bf16[576,1536]{1,0:T(8,128)(2,1)} %param.25) | copy-start | bytes 5308420
  6.5 55.7 %copy-start.8 = (bf16[1536,128]{1,0:T(8,128)(2,1)S(1)}, bf16[1536,128]{1,0:T(8,128)(2,1)}, u32[]{:S(2)}) copy-start(bf16[1536,128]{1,0:T(8,128)(2,1)} %param.18) | copy-start | bytes 1179652
  6.5 345.9 %reduce-scatter.6.cloned.1.call-start = ((), (), s32[]{:S(2)}) async-start(), calls=%async_computation.2 | async-start | bytes 540672
  61.3 27.5 %copy-start.2 = (f32[32,1536]{1,0:T(8,128)}, f32[32,1536]{1,0:T(8,128)S(1)}, u32[]{:S(2)}) copy-start(f32[32,1536]{1,0:T(8,128)S(1)} %reshape.246) | copy-start | bytes 589828
  62.2 158.5 %copy-start.6 = (bf16[32,1536]{1,0:T(8,128)(2,1)}, bf16[32,1536]{1,0:T(8,128)(2,1)S(1)}, u32[]{:S(2)}) copy-start(bf16[32,1536]{1,0:T(8,128)(2,1)S(1)} %multiply_convert_fusion) | copy-start | bytes 294916
  213.1 0.6 copy-start.7
  216.2 4.5 copy-start.9
  220.6 245.2 %all-reduce.4.cloned.1.call-start = ((), (), s32[]{:S(2)}) async-start(), calls=%async_computation.1 | async-start | bytes 196608 | tf_op jit(solution)/shard_map/psum | solution.py:144
  224.2 163.0 %copy-start.1 = (bf16[1536,576]{0,1:T(8,128)(2,1)S(1)}, bf16[1536,576]{0,1:T(8,128)(2,1)}, u32[]{:S(2)}) copy-start(bf16[1536,576]{0,1:T(8,128)(2,1)} %param.23) | copy-start | bytes 5308420
  224.2 163.0 %copy-start.10 = (f32[1536]{0:T(1024)S(1)}, f32[1536]{0:T(1024)}, u32[]{:S(2)}) copy-start(f32[1536]{0:T(1024)} %param.22) | copy-start | bytes 18436
  353.8 32.6 %copy-start.3 = (f32[32,1536]{1,0:T(8,128)S(1)}, f32[32,1536]{1,0:T(8,128)}, u32[]{:S(2)}) copy-start(f32[32,1536]{1,0:T(8,128)} %copy-done.2) | copy-start | bytes 589828
  355.9 7.4 %collective-permute-start = (f32[32,1536]{1,0:T(8,128)S(1)}, f32[32,1536]{1,0:T(8,128)S(1)}, u32[]{:S(2)}, u32[]{:S(2)}) collective-permute-start(f32[32,1536]{1,0:T(8,128)S(1)} %fusion.66), channel_id=1, source_target_pairs={{0,1},{1,0},{2,3},{3,2},{4,5},{5,4},{6,7},{7,6},{8,9},{9,8},{10,11... | collective-permute-start | bytes 589832 | tf_op jit(solution)/shard_map/ppermute | solution.py:135
  363.3 13.0 %collective-permute-start.1 = (f32[32,1536]{1,0:T(8,128)S(1)}, f32[32,1536]{1,0:T(8,128)S(1)}, u32[]{:S(2)}, u32[]{:S(2)}) collective-permute-start(f32[32,1536]{1,0:T(8,128)S(1)} %add.144), channel_id=1, source_target_pairs={{0,2},{1,3},{2,0},{3,1},{4,6},{5,7},{6,4},{7,5},{8,10},{9,11},{10,... | collective-permute-start | bytes 589832 | tf_op jit(solution)/shard_map/ppermute | solution.py:135
  376.3 10.0 %collective-permute-start.2 = (f32[32,1536]{1,0:T(8,128)S(1)}, f32[32,1536]{1,0:T(8,128)S(1)}, u32[]{:S(2)}, u32[]{:S(2)}) collective-permute-start(f32[32,1536]{1,0:T(8,128)S(1)} %add.145), channel_id=1, source_target_pairs={{0,4},{1,5},{2,6},{3,7},{4,0},{5,1},{6,2},{7,3},{8,12},{9,13},{10,... | collective-permute-start | bytes 589832 | tf_op jit(solution)/shard_map/ppermute | solution.py:135
  386.5 0.6 copy-start.4
  388.5 77.3 %copy-start.5 = (bf16[32,1536]{1,0:T(8,128)(2,1)S(1)}, bf16[32,1536]{1,0:T(8,128)(2,1)}, u32[]{:S(2)}) copy-start(bf16[32,1536]{1,0:T(8,128)(2,1)} %copy-done.4) | copy-start | bytes 294916
Sparse Core Ops, SparseCore 0:
  220.8 87.7 reduce-scatter.5
  391.8 73.9 all-reduce.3
